TPU v7x, 128 devices: a whole 4x4x4 slice. The times are simulated.
128 devices in a mesh: req: 16 (over y, x), head: 8 (over z, core).
Axes of the slice: x: 4, y: 4, z: 4, core: 2. Of those that a mesh axis runs over, the one named last changes fastest.
Arguments:
- hidden_in: bfloat16 [4864, 3072], P('req', 'head'), may hold values from -6 to 6
- dec_query: bfloat16 [768, 3072], P('req', 'head'), may hold values from -5.5 to 5.5
- dec_key: bfloat16 [768, 3072], P('req', 'head'), may hold values from -6 to 6
- dec_value: bfloat16 [768, 3072], P('req', 'head'), may hold values from -6 to 6
- pre_query: bfloat16 [4096, 3072], P('req', 'head'), may hold values from -5.5 to 5.5
- pre_key: bfloat16 [4096, 3072], P('req', 'head'), may hold values from -6 to 6
- pre_value: bfloat16 [4096, 3072], P('req', 'head'), may hold values from -6 to 6
- cache_key: bfloat16 [32, 2048, 3072], P('req', None, 'head'), may hold values from -5.5 to 5.5
- cache_value: bfloat16 [32, 2048, 3072], P('req', None, 'head'), may hold values from -6 to 6
- group_of: int32 [768, 1], replicated, may hold values from 0 to 31; in each aligned block of 768 rows (0 to 767, 768 to 1535, ...) at most 48 rows name the same one
- cache_length: int32 [32], P('req'), may hold values from 256 to 2048, as said below
- stretch_start: int32 [16], P('req'), may hold values from 256 to 2048, as said below
- row_owner: int32 [4864, 1], P('req'), may hold values from 0 to 15; in each aligned block of 304 rows (0 to 303, 304 to 607, ...) at most 40 rows name the same one
- out_weight: bfloat16 [3072, 3072], P('head'), may hold values from -0.109375 to 0.109375
- norm_gain: float32 [3072], replicated, may hold values from 0.1 to 1.9
- gate_weight: bfloat16 [3072, 4096], P(None, 'head'), may hold values from -0.109375 to 0.109375
- up_weight: bfloat16 [3072, 4096], P(None, 'head'), may hold values from -0.109375 to 0.109375
- down_weight: bfloat16 [4096, 3072], P('head'), may hold values from -0.09375 to 0.09375
Outputs:
- layer_out: bfloat16 [10240, 3072], P(('req', 'head'))
Inputs may be any that keep to these rules, and one draw needn't show every extreme that they name: `group_of`: at most 48 requests share a cache group, exactly 48 in some group; every group has a request. `cache_length`: some group has all 2048 rows valid. `stretch_start`: some stretch follows all 2048 cached rows. `row_owner`: among the 304 rows of one index of req at most 40 share an owner, exactly 40 on some index.
All inputs are finite; a program needn't handle non-finite values.
Results may differ from a plain program's by a relative error of at most 0.02.
Values may be sent and summed in bfloat16 or wider, within the bound.
No kernel may reach another device: no remote copies, remote signals or barrier semaphores. Data moves between devices by JAX's collectives and lax.ppermute only.
A program may use at most 128 MiB of HBM per device.

v0:
```python
import math

import jax
import jax.numpy as jnp
from jax import lax
from jax.sharding import PartitionSpec as P

HD = 96
CAP = 48


eps_norm = 1e-05


def head_split(matrix):
    return matrix.reshape(matrix.shape[0], matrix.shape[1] // HD, HD)


def softmax_rows(scores, allowed):
    masked = jnp.where(allowed, scores, -jnp.inf)
    highest = jnp.max(masked, axis=-1, keepdims=True)
    raised = jnp.exp(masked - highest)
    return (raised / jnp.sum(raised, axis=-1, keepdims=True)).astype(jnp.bfloat16)


def on_device(
    hidden_in,
    dec_query,
    dec_key,
    dec_value,
    pre_query,
    pre_key,
    pre_value,
    cache_key,
    cache_value,
    group_of,
    cache_length,
    stretch_start,
    row_owner,
    out_weight,
    norm_gain,
    gate_weight,
    up_weight,
    down_weight,
):
    factor = 1.0 / math.sqrt(HD)
    width_here = dec_query.shape[1]
    queries_all, keys_own, values_own = (
        lax.all_gather(dec_query, "req", axis=0, tiled=True),
        lax.all_gather(dec_key, "req", axis=0, tiled=True),
        lax.all_gather(dec_value, "req", axis=0, tiled=True),
    )
    groups_here = cache_key.shape[0]
    length_cache = cache_key.shape[1]
    first_group = lax.axis_index("req") * groups_here
    members = group_of[:, 0]
    wanted = first_group + jnp.arange(groups_here, dtype=jnp.int32)
    belongs = (members[None, :] == wanted[:, None]).astype(jnp.int32)
    ranking = jnp.cumsum(belongs, axis=1) - 1
    places = jnp.arange(CAP, dtype=jnp.int32)
    chosen = (belongs[:, None, :] == 1) & (ranking[:, None, :] == places[None, :, None])
    chooser = chosen.reshape(groups_here * CAP, members.shape[0])
    stacked_in = jnp.concatenate([queries_all, keys_own, values_own], axis=1)
    picked = jnp.dot(
        chooser.astype(jnp.bfloat16), stacked_in, preferred_element_type=jnp.float32
    ).astype(jnp.bfloat16)
    positions = jnp.arange(length_cache)
    results = []
    for group_pos in range(groups_here):
        rows_block = picked[group_pos * CAP : (group_pos + 1) * CAP]
        picked_q = head_split(rows_block[:, :width_here])
        picked_k = head_split(rows_block[:, width_here : 2 * width_here])
        picked_v = head_split(rows_block[:, 2 * width_here :])
        cache_scores = (
            jnp.einsum(
                "qhd,khd->hqk",
                picked_q,
                head_split(cache_key[group_pos]),
                preferred_element_type=jnp.float32,
            )
            * factor
        )
        own_scores = (
            jnp.sum(picked_q.astype(jnp.float32) * picked_k.astype(jnp.float32), axis=-1).T * factor
        )
        scores = jnp.concatenate([cache_scores, own_scores[:, :, None]], axis=-1)
        allowed = jnp.concatenate([positions < cache_length[group_pos], jnp.ones((1,), bool)])[
            None, None, :
        ]
        weights = softmax_rows(scores, allowed)
        blended = jnp.einsum(
            "hqk,khd->qhd",
            weights[:, :, :length_cache],
            head_split(cache_value[group_pos]),
            preferred_element_type=jnp.float32,
        )
        blended = blended + weights[:, :, length_cache].astype(jnp.float32).T[
            :, :, None
        ] * picked_v.astype(jnp.float32)
        results.append(blended.reshape(CAP, width_here))
    stacked = jnp.concatenate(results, axis=0)
    spread_back = jnp.dot(chooser.astype(jnp.float32).T, stacked, precision=lax.Precision.HIGHEST)
    dec_out = lax.psum_scatter(
        spread_back.astype(jnp.bfloat16), "req", scatter_dimension=0, tiled=True
    )
    stretch_len = pre_query.shape[0]
    key_rows = jnp.concatenate([cache_key[0], pre_key], axis=0)
    value_rows = jnp.concatenate([cache_value[0], pre_value], axis=0)
    columns = jnp.arange(length_cache + stretch_len)
    row_numbers = jnp.arange(stretch_len)
    allowed_pre = jnp.where(
        columns[None, :] < length_cache,
        columns[None, :] < stretch_start[0],
        columns[None, :] - length_cache <= row_numbers[:, None],
    )
    pre_scores = (
        jnp.einsum(
            "qhd,khd->hqk",
            head_split(pre_query),
            head_split(key_rows),
            preferred_element_type=jnp.float32,
        )
        * factor
    )
    pre_weights = softmax_rows(pre_scores, allowed_pre[None])
    pre_mixed = jnp.einsum(
        "hqk,khd->qhd", pre_weights, head_split(value_rows), preferred_element_type=jnp.float32
    )
    pre_out = pre_mixed.reshape(stretch_len, width_here).astype(jnp.bfloat16)
    attn_rows = jnp.concatenate([dec_out, pre_out], axis=0)
    projected = jnp.dot(attn_rows, out_weight, preferred_element_type=jnp.float32)
    col_start = lax.axis_index("head") * width_here
    own_cols = lax.dynamic_slice_in_dim(projected, col_start, width_here, 1) + hidden_in.astype(
        jnp.float32
    )
    contribution = lax.dynamic_update_slice_in_dim(projected, own_cols, col_start, 1)
    req_count = lax.axis_size("req")
    row_count = contribution.shape[0]
    slot_rows = 8 * ((2 * row_count + 8 * req_count - 1) // (8 * req_count))
    owners = row_owner[:, 0]
    onehot_owner = (owners[:, None] == jnp.arange(req_count, dtype=jnp.int32)[None, :]).astype(
        jnp.int32
    )
    before = jnp.sum((jnp.cumsum(onehot_owner, axis=0) - 1) * onehot_owner, axis=1)
    target = owners * slot_rows + before
    placing = (
        target[None, :] == jnp.arange(req_count * slot_rows, dtype=jnp.int32)[:, None]
    ).astype(jnp.bfloat16)
    residual = lax.psum(contribution.astype(jnp.bfloat16), "head")
    outgoing = jnp.dot(placing, residual, preferred_element_type=jnp.float32).astype(jnp.bfloat16)
    arrived = lax.all_to_all(outgoing, "req", split_axis=0, concat_axis=0, tiled=True)
    arrived_wide = arrived.astype(jnp.float32)
    squares = jnp.mean(jnp.square(arrived_wide), axis=-1, keepdims=True)
    normed = (arrived_wide * lax.rsqrt(squares + eps_norm) * norm_gain).astype(jnp.bfloat16)
    gate_act = jnp.dot(normed, gate_weight, preferred_element_type=jnp.float32)
    up_act = jnp.dot(normed, up_weight, preferred_element_type=jnp.float32)
    hidden = (jax.nn.silu(gate_act) * up_act).astype(jnp.bfloat16)
    rows_here = arrived.shape[0] // lax.axis_size("head")
    down_sum = lax.psum_scatter(
        jnp.dot(hidden, down_weight, preferred_element_type=jnp.float32).astype(jnp.bfloat16),
        "head",
        scatter_dimension=0,
        tiled=True,
    ).astype(jnp.float32)
    own_rows = lax.dynamic_slice_in_dim(
        arrived_wide, lax.axis_index("head") * rows_here, rows_here, 0
    )
    return (own_rows + down_sum).astype(jnp.bfloat16)


def solution(mesh):
    placed = (
        P("req", "head"),
        P("req", "head"),
        P("req", "head"),
        P("req", "head"),
        P("req", "head"),
        P("req", "head"),
        P("req", "head"),
        P("req", None, "head"),
        P("req", None, "head"),
        P(),
        P("req"),
        P("req"),
        P("req", None),
        P("head", None),
        P(),
        P(None, "head"),
        P(None, "head"),
        P("head", None),
    )
    return jax.shard_map(
        on_device, mesh=mesh, in_specs=placed, out_specs=P(("req", "head"), None), check_vma=False
    )
```

profile of v0, /device:TPU:1, one launch (start us, length us, event | category | flops | bytes accessed | tf_op | source)
XLA Modules:
  0.0 388.0 jit_solution(7005297331430344854)
XLA Ops:
  6.6 1.5 fusion.83
  8.8 1.3 iota_compare_fusion.7
  11.9 20.1 %all_gather.9 = bf16[768,384]{1,0:T(8,128)(2,1)S(1)} all-gather(bf16[48,384]{1,0:T(8,128)(2,1)} %param.19), channel_id=1, replica_groups=mesh['req'=16,'head'=8] {'req'}, dimensions={0}, use_global_device_ids=true | all-gather | bytes 626688 | tf_op jit(solution)/shard_map/all_gather | solution.py:49
  32.0 17.6 %all_gather.10 = bf16[768,384]{1,0:T(8,128)(2,1)S(1)} all-gather(bf16[48,384]{1,0:T(8,128)(2,1)} %param.20), channel_id=1, replica_groups=mesh['req'=16,'head'=8] {'req'}, dimensions={0}, use_global_device_ids=true | all-gather | bytes 626688 | tf_op jit(solution)/shard_map/all_gather | solution.py:50
  49.6 17.8 %all_gather.11 = bf16[768,384]{1,0:T(8,128)(2,1)S(1)} all-gather(bf16[48,384]{1,0:T(8,128)(2,1)} %param.21), channel_id=1, replica_groups=mesh['req'=16,'head'=8] {'req'}, dimensions={0}, use_global_device_ids=true | all-gather | bytes 626688 | tf_op jit(solution)/shard_map/all_gather | solution.py:51
  75.2 3.9 fusion.81
  79.0 2.6 copy.77
  81.7 1.8 convolution_multiply_fusion
  85.2 2.6 copy.70
  87.8 1.8 convolution_multiply_fusion.1
  91.7 1.9 fusion.82
  93.7 2.6 copy.81
  96.3 2.3 fusion.31
  98.8 2.7 copy.74
  101.4 2.3 fusion.32
  103.9 1.5 convolution_convert_fusion.3
  109.1 1.7 copy.84
  110.9 3.8 fusion.12
  114.6 4.9 %fusion.84 = f32[4,256]{1,0:T(4,128)S(1)} fusion(pred[256,2304]{0,1:T(8,128)(4,1)} %fusion.12, bf16[256,4,96]{0,2,1:T(8,128)(2,1)S(1)} %bitcast.97, bf16[256,4,96]{0,2,1:T(8,128)(2,1)S(1)} %bitcast.99, bf16[2048,4,96]{0,2,1:T(8,128)(2,1)} %bitcast.90), kind=kOutput, calls=%fused_computation.125 | convolution fusion | flops 465963264 | bytes 2560000 | tf_op jit(solution)/shard_map/sub | solution.py:22
  119.5 7.6 %fusion.28 = bf16[4,96,256]{2,1,0:T(8,128)(2,1)} fusion(f32[4,256]{1,0:T(4,128)S(1)} %fusion.84, bf16[256,4,96]{0,2,1:T(8,128)(2,1)} %bitcast.101, bf16[2048,4,96]{0,2,1:T(8,128)(2,1)} %bitcast.93, pred[256,2304]{0,1:T(8,128)(4,1)} %fusion.12, bf16[256,4,96]{0,2,1:T(8,128)(2,1)S(1)} %bitcast.98, bf16[256,4,96]{0,2,1:T(8,128)(2,1)S(1)} %bitcast.100, ...), kind=kOutput, calls=%fused_computation.45 | convolution fusion | flops 924945664 | bytes 4526080 | tf_op jit(solution)/shard_map/hqk,khd->qhd/dot_general | solution.py:126
  127.1 65.0 %reduce-scatter.7.cloned.1.call-done = bf16[48,384]{1,0:T(8,128)(2,1)} async-done(((bf16[768,384]{1,0:T(8,128)(2,1)}), bf16[48,384]{1,0:T(8,128)(2,1)}) %reduce-scatter.7.cloned.1.call-update) | async-done | bytes 36880
  193.0 3.1 fusion.44
  196.2 1.5 convert_element_type.133
  199.2 62.9 %all-reduce.4.cloned.1.call-done = bf16[304,3072]{1,0:T(8,128)(2,1)} async-done(((bf16[304,3072]{1,0:T(8,128)(2,1)}), bf16[304,3072]{1,0:T(8,128)(2,1)}) %all-reduce.4.cloned.1.call-update) | async-done | bytes 1867792 | tf_op jit(solution)/shard_map/psum | solution.py:149
  262.2 3.7 convolution_convert_fusion.1
  265.9 51.8 %all_to_all.9 = bf16[16,40,3072]{2,1,0:T(8,128)(2,1)S(1)} all-to-all(bf16[16,40,3072]{2,1,0:T(8,128)(2,1)S(1)} %bitcast.96), channel_id=1, replica_groups=mesh['req'=16,'head'=8] {'req'}, dimensions={0} | all-to-all | bytes 7864320 | tf_op jit(solution)/shard_map/all_to_all | solution.py:151
  319.8 6.9 %multiply_convert_fusion = (bf16[640,3072]{1,0:T(8,128)(2,1)S(1)}, f32[16,40,3072]{2,1,0:T(8,128)}) fusion(f32[3072]{0:T(1024)S(1)} %copy-done.10, f32[640]{0:T(1024)S(1)} %rsqrt.12, bf16[16,40,3072]{2,1,0:T(8,128)(2,1)} %copy-done.1), kind=kLoop, calls=%fused_computation.7 | loop fusion | flops 7864320 | bytes 15743488 | tf_op jit(solution)/shard_map/convert_element_type | solution.py:154
  326.7 2.0 copy-done.2
  328.7 3.2 fusion.89
  332.0 9.7 %convolution_convert_fusion = bf16[640,3072]{1,0:T(8,128)(2,1)} fusion(bf16[512,3072]{1,0:T(8,128)(2,1)S(1)} %copy-done, bf16[640,3072]{1,0:T(8,128)(2,1)} %copy-done.2, bf16[3072,512]{1,0:T(8,128)(2,1)} %param.34, f32[640,512]{1,0:T(8,128)} %fusion.89), kind=kOutput, calls=%fused_computation.9 | convolution fusion | flops 4030464000 | bytes 15466496 | tf_op jit(solution)/shard_map/dot_general | solution.py:160
  341.7 37.6 %reduce-scatter.5.cloned.1.call-done = bf16[80,3072]{1,0:T(8,128)(2,1)} async-done(((bf16[640,3072]{1,0:T(8,128)(2,1)}), bf16[80,3072]{1,0:T(8,128)(2,1)}) %reduce-scatter.5.cloned.1.call-update) | async-done | bytes 491536 | tf_op jit(solution)/shard_map/reduce_scatter | solution.py:159
  379.3 2.2 add_convert_fusion
  (89 shorter events, 22.0 us)
Async XLA Ops:
  6.5 325.4 %copy-start = (bf16[512,3072]{1,0:T(8,128)(2,1)S(1)}, bf16[512,3072]{1,0:T(8,128)(2,1)}, u32[]{:S(2)}) copy-start(bf16[512,3072]{1,0:T(8,128)(2,1)} %param.35) | copy-start | bytes 9437188
  6.5 185.6 %reduce-scatter.7.cloned.1.call-start = ((), (), s32[]{:S(2)}) async-start(), calls=%async_computation.5 | async-start | bytes 626688
  67.6 0.6 copy-start.6
  81.7 1.8 copy-start.11
  81.7 1.8 copy-start.9
  84.2 0.9 copy-start.3
  89.5 2.2 copy-start.5
  90.2 0.9 copy-start.4
  101.4 2.5 copy-start.7
  101.4 4.9 %copy-start.12 = (s32[304,1]{0,1:T(1,128)S(1)}, s32[304,1]{0,1:T(1,128)}, u32[]{:S(2)}) copy-start(s32[304,1]{0,1:T(1,128)} %param.30) | copy-start | bytes 3652
  105.5 156.7 %all-reduce.4.cloned.1.call-start = ((), (), s32[]{:S(2)}) async-start(), calls=%async_computation.3 | async-start | bytes 3735552 | tf_op jit(solution)/shard_map/psum | solution.py:149
  193.0 3.1 copy-start.8
  197.7 181.6 %reduce-scatter.5.cloned.1.call-start = ((), (), s32[]{:S(2)}) async-start(), calls=%async_computation.4 | async-start | bytes 4423680 | tf_op jit(solution)/shard_map/reduce_scatter | solution.py:159
  317.7 2.0 copy-start.1
  317.7 2.1 copy-start.10
  319.8 8.9 %copy-start.13 = (bf16[3072,512]{1,0:T(8,128)(2,1)S(1)}, bf16[3072,512]{1,0:T(8,128)(2,1)}, u32[]{:S(2)}) copy-start(bf16[3072,512]{1,0:T(8,128)(2,1)} %param.33) | copy-start | bytes 9437188
  326.7 2.0 copy-start.2
Sparse Core Ops, SparseCore 0:
  105.6 86.4 reduce-scatter.6
  197.8 64.3 all-reduce.3
  341.8 37.4 reduce-scatter.4
where the time goes:
time: 392 us; the launch traced here: 388 us
  waiting for transfers between devices  166 us (42%)
  blocking collectives  107 us (27%)
  matrix products  42.3 us (11%)
  local copies, waits for them, and re-layouts  34.5 us (9%)
  other arithmetic  23.7 us (6%)
  between operations  14.1 us (4%)
    unnamed x4, waiting for transfers between devices  65 us
    psum x1, waiting for transfers between devices, on_device(): residual = lax.psum(contribution.astype(jnp.bfloat16), 'head')  62.9 us
    all_to_all x1, blocking collectives, on_device(): lax.all_to_all(outgoing, 'req', split_axis=0, concat_axis=0, tiled=True)  51.8 us
    reduce_scatter x1, waiting for transfers between devices, on_device(): lax.psum_scatter(jnp.dot(hidden, down_weight, preferred_element_type=jnp....  37.6 us
    all_gather x1, blocking collectives, on_device(): lax.all_gather(dec_query, 'req', axis=0, tiled=True)  20.1 us
    all_gather x1, blocking collectives, on_device(): lax.all_gather(dec_value, 'req', axis=0, tiled=True)  17.8 us
    all_gather x1, blocking collectives, on_device(): lax.all_gather(dec_key, 'req', axis=0, tiled=True)  17.6 us
    dot_general x1, matrix products, on_device(): jnp.dot(hidden, down_weight, preferred_element_type=jnp.float32)  9.69 us
  transfers between devices with their start and end apart: 3, of which 3 were waited for; matrix products, arithmetic and copies ran while one was open for 6% of the time, Pallas kernels for 0%

commit v1 on v0

--- a/solution.py
+++ b/solution.py
@@ -21,6 +21,10 @@
     highest = jnp.max(masked, axis=-1, keepdims=True)
     raised = jnp.exp(masked - highest)
     return (raised / jnp.sum(raised, axis=-1, keepdims=True)).astype(jnp.bfloat16)
+
+
+def rank_within(onehot, axis):
+    return jnp.sum((jnp.cumsum(onehot, axis=axis) - 1) * onehot, axis=-1)
 
 
 def on_device(
@@ -45,24 +49,45 @@
 ):
     factor = 1.0 / math.sqrt(HD)
     width_here = dec_query.shape[1]
-    queries_all, keys_own, values_own = (
-        lax.all_gather(dec_query, "req", axis=0, tiled=True),
-        lax.all_gather(dec_key, "req", axis=0, tiled=True),
-        lax.all_gather(dec_value, "req", axis=0, tiled=True),
-    )
+    req_count = lax.axis_size("req")
+    head_count = lax.axis_size("head")
+    me = lax.axis_index("req")
     groups_here = cache_key.shape[0]
     length_cache = cache_key.shape[1]
-    first_group = lax.axis_index("req") * groups_here
+    per_home = dec_query.shape[0]
     members = group_of[:, 0]
+    total_reqs = members.shape[0]
+
+    holder_of = members // groups_here
+    holder_hot = (holder_of[:, None] == jnp.arange(req_count, dtype=jnp.int32)[None, :]).astype(jnp.int32)
+    rank_all = rank_within(holder_hot.reshape(req_count, per_home, req_count), 1).reshape(total_reqs)
+    slot_of = (jnp.arange(total_reqs, dtype=jnp.int32) // per_home) * per_home + rank_all
+
+    my_holder = lax.dynamic_slice_in_dim(holder_of, me * per_home, per_home)
+    my_rank = lax.dynamic_slice_in_dim(rank_all, me * per_home, per_home)
+    my_slot = my_holder * per_home + my_rank
+    packer = (
+        my_slot[None, :] == jnp.arange(req_count * per_home, dtype=jnp.int32)[:, None]
+    ).astype(jnp.bfloat16)
+    stacked_in = jnp.concatenate([dec_query, dec_key, dec_value], axis=1)
+    outgoing_q = jnp.dot(packer, stacked_in, preferred_element_type=jnp.float32).astype(jnp.bfloat16)
+    arrived_q = lax.all_to_all(outgoing_q, "req", split_axis=0, concat_axis=0, tiled=True)
+
+    first_group = me * groups_here
     wanted = first_group + jnp.arange(groups_here, dtype=jnp.int32)
     belongs = (members[None, :] == wanted[:, None]).astype(jnp.int32)
     ranking = jnp.cumsum(belongs, axis=1) - 1
     places = jnp.arange(CAP, dtype=jnp.int32)
-    chosen = (belongs[:, None, :] == 1) & (ranking[:, None, :] == places[None, :, None])
-    chooser = chosen.reshape(groups_here * CAP, members.shape[0])
-    stacked_in = jnp.concatenate([queries_all, keys_own, values_own], axis=1)
+    chosen = ((belongs[:, None, :] == 1) & (ranking[:, None, :] == places[None, :, None])).reshape(
+        groups_here * CAP, total_reqs
+    )
+    chosen_slot = jnp.sum(jnp.where(chosen, slot_of[None, :], 0), axis=1)
+    chosen_any = jnp.any(chosen, axis=1)
+    chooser = chosen_any[:, None] & (
+        chosen_slot[:, None] == jnp.arange(req_count * per_home, dtype=jnp.int32)[None, :]
+    )
     picked = jnp.dot(
-        chooser.astype(jnp.bfloat16), stacked_in, preferred_element_type=jnp.float32
+        chooser.astype(jnp.bfloat16), arrived_q, preferred_element_type=jnp.float32
     ).astype(jnp.bfloat16)
     positions = jnp.arange(length_cache)
     results = []
@@ -98,11 +123,13 @@
             :, :, None
         ] * picked_v.astype(jnp.float32)
         results.append(blended.reshape(CAP, width_here))
-    stacked = jnp.concatenate(results, axis=0)
-    spread_back = jnp.dot(chooser.astype(jnp.float32).T, stacked, precision=lax.Precision.HIGHEST)
-    dec_out = lax.psum_scatter(
-        spread_back.astype(jnp.bfloat16), "req", scatter_dimension=0, tiled=True
-    )
+    stacked = jnp.concatenate(results, axis=0).astype(jnp.bfloat16)
+    going_back = jnp.dot(
+        chooser.astype(jnp.bfloat16).T, stacked, preferred_element_type=jnp.float32
+    ).astype(jnp.bfloat16)
+    came_back = lax.all_to_all(going_back, "req", split_axis=0, concat_axis=0, tiled=True)
+    dec_out = jnp.dot(packer.T, came_back, preferred_element_type=jnp.float32).astype(jnp.bfloat16)
+
     stretch_len = pre_query.shape[0]
     key_rows = jnp.concatenate([cache_key[0], pre_key], axis=0)
     value_rows = jnp.concatenate([cache_value[0], pre_value], axis=0)
@@ -129,43 +156,39 @@
     pre_out = pre_mixed.reshape(stretch_len, width_here).astype(jnp.bfloat16)
     attn_rows = jnp.concatenate([dec_out, pre_out], axis=0)
     projected = jnp.dot(attn_rows, out_weight, preferred_element_type=jnp.float32)
-    col_start = lax.axis_index("head") * width_here
+    head_me = lax.axis_index("head")
+    col_start = head_me * width_here
     own_cols = lax.dynamic_slice_in_dim(projected, col_start, width_here, 1) + hidden_in.astype(
         jnp.float32
     )
     contribution = lax.dynamic_update_slice_in_dim(projected, own_cols, col_start, 1)
-    req_count = lax.axis_size("req")
-    row_count = contribution.shape[0]
+    residual = lax.psum(contribution.astype(jnp.bfloat16), "head")
+
+    residual_wide = residual.astype(jnp.float32)
+    squares = jnp.mean(jnp.square(residual_wide), axis=-1, keepdims=True)
+    normed = (residual_wide * lax.rsqrt(squares + eps_norm) * norm_gain).astype(jnp.bfloat16)
+    gate_act = jnp.dot(normed, gate_weight, preferred_element_type=jnp.float32)
+    up_act = jnp.dot(normed, up_weight, preferred_element_type=jnp.float32)
+    hidden = (jax.nn.silu(gate_act) * up_act).astype(jnp.bfloat16)
+    down_part = jnp.dot(hidden, down_weight, preferred_element_type=jnp.float32).astype(jnp.bfloat16)
+    down_cols = lax.psum_scatter(down_part, "head", scatter_dimension=1, tiled=True)
+    own_residual = lax.dynamic_slice_in_dim(residual_wide, col_start, width_here, 1)
+    out_cols = (own_residual + down_cols.astype(jnp.float32)).astype(jnp.bfloat16)
+
+    row_count = residual.shape[0]
     slot_rows = 8 * ((2 * row_count + 8 * req_count - 1) // (8 * req_count))
     owners = row_owner[:, 0]
     onehot_owner = (owners[:, None] == jnp.arange(req_count, dtype=jnp.int32)[None, :]).astype(
         jnp.int32
     )
-    before = jnp.sum((jnp.cumsum(onehot_owner, axis=0) - 1) * onehot_owner, axis=1)
+    before = rank_within(onehot_owner, 0)
     target = owners * slot_rows + before
     placing = (
         target[None, :] == jnp.arange(req_count * slot_rows, dtype=jnp.int32)[:, None]
     ).astype(jnp.bfloat16)
-    residual = lax.psum(contribution.astype(jnp.bfloat16), "head")
-    outgoing = jnp.dot(placing, residual, preferred_element_type=jnp.float32).astype(jnp.bfloat16)
+    outgoing = jnp.dot(placing, out_cols, preferred_element_type=jnp.float32).astype(jnp.bfloat16)
     arrived = lax.all_to_all(outgoing, "req", split_axis=0, concat_axis=0, tiled=True)
-    arrived_wide = arrived.astype(jnp.float32)
-    squares = jnp.mean(jnp.square(arrived_wide), axis=-1, keepdims=True)
-    normed = (arrived_wide * lax.rsqrt(squares + eps_norm) * norm_gain).astype(jnp.bfloat16)
-    gate_act = jnp.dot(normed, gate_weight, preferred_element_type=jnp.float32)
-    up_act = jnp.dot(normed, up_weight, preferred_element_type=jnp.float32)
-    hidden = (jax.nn.silu(gate_act) * up_act).astype(jnp.bfloat16)
-    rows_here = arrived.shape[0] // lax.axis_size("head")
-    down_sum = lax.psum_scatter(
-        jnp.dot(hidden, down_weight, preferred_element_type=jnp.float32).astype(jnp.bfloat16),
-        "head",
-        scatter_dimension=0,
-        tiled=True,
-    ).astype(jnp.float32)
-    own_rows = lax.dynamic_slice_in_dim(
-        arrived_wide, lax.axis_index("head") * rows_here, rows_here, 0
-    )
-    return (own_rows + down_sum).astype(jnp.bfloat16)
+    return lax.all_to_all(arrived, "head", split_axis=0, concat_axis=1, tiled=True)
 
 
 def solution(mesh):

time: 392 us -> 254 us (0.65)
  blocking collectives: 107 us -> 32.6 us
  waiting for transfers between devices: 166 us -> 93.8 us
  starting transfers between devices: 0.49 us -> 14.8 us
  other arithmetic: 23.7 us -> 19.5 us
    all_gather x3 -> x0, blocking collectives: 55.5 us -> none  [the longest x1 20.1 us: on_device(): lax.all_gather(dec_query, 'req', axis=0, tiled=True)]
    unnamed x4 -> x3, waiting for transfers between devices: 65 us -> 27.4 us
    reduce_scatter x1 -> x0, waiting for transfers between devices: 37.6 us -> none  [on_device(): lax.psum_scatter(jnp.dot(hidden, down_weight, preferred_element_type=jnp....]
    all_to_all x1, blocking collectives: 51.8 us -> 15.3 us  [on_device(): lax.all_to_all(outgoing, 'req', split_axis=0, concat_axis=0, tiled=True)]
    all_to_all x0 -> x1, blocking collectives: none -> 17.3 us  [on_device(): lax.all_to_all(arrived, 'head', split_axis=0, concat_axis=1, tiled=True)]
    all_to_all x0 -> x2, starting transfers between devices: none -> 14.3 us  [the longest x1 7.62 us: on_device(): lax.all_to_all(outgoing_q, 'req', split_axis=0, concat_axis=0, tiled=True)]
    convert_element_type x2 -> x1, other arithmetic: 9.16 us -> 3.76 us  [on_device(): residual_wide = residual.astype(jnp.float32)]
    dot_general x3 -> x5, matrix products: 5.6 us -> 8.64 us  [the longest x1 2.61 us: on_device(): jnp.dot(packer, stacked_in, preferred_element_type=jnp.float32)]
  transfers between devices with their start and end apart: 3 -> 4, of which waited for: 3 -> 2; matrix products, arithmetic and copies ran while one was open for 6% -> 18% of each run, Pallas kernels for 0% -> 0%
where the time goes in v1:
time: 254 us; the launch traced here: 253 us
  waiting for transfers between devices  93.8 us (37%)
  matrix products  42.6 us (17%)
  local copies, waits for them, and re-layouts  35.4 us (14%)
  blocking collectives  32.6 us (13%)
  other arithmetic  19.5 us (8%)
  starting transfers between devices  14.8 us (6%)
  between operations  14.5 us (6%)
    psum x1, waiting for transfers between devices, on_device(): residual = lax.psum(contribution.astype(jnp.bfloat16), 'head')  66.4 us
    unnamed x3, waiting for transfers between devices  27.4 us
    all_to_all x1, blocking collectives, on_device(): lax.all_to_all(arrived, 'head', split_axis=0, concat_axis=1, tiled=True)  17.3 us
    all_to_all x1, blocking collectives, on_device(): lax.all_to_all(outgoing, 'req', split_axis=0, concat_axis=0, tiled=True)  15.3 us
    unnamed x42, local copies, waits for them, and re-layouts  11.1 us
    slice x3, local copies, waits for them, and re-layouts, on_device(): cache_value[group_pos]  9.26 us
    slice x3, local copies, waits for them, and re-layouts, on_device(): cache_key[group_pos]  9.16 us
    dot_general x1, matrix products, on_device(): jnp.einsum('hqk,khd->qhd', pre_weights, head_split(value_rows), preferred...  7.65 us
  transfers between devices with their start and end apart: 4, of which 2 were waited for; matrix products, arithmetic and copies ran while one was open for 18% of the time, Pallas kernels for 0%

profile of v1, /device:TPU:1, one launch (start us, length us, event | category | flops | bytes accessed | tf_op | source)
XLA Modules:
  0.0 253.0 jit_solution(7330555277731278193)
XLA Ops:
  8.9 2.6 %convolution_convert_fusion.1 = bf16[768,1152]{1,0:T(8,128)(2,1)} fusion(s32[48]{0:T(128)S(1)} %dynamic-slice_add_fusion, bf16[48,384]{1,0:T(8,128)(2,1)} %param.21, bf16[48,384]{1,0:T(8,128)(2,1)} %param.20, bf16[48,384]{1,0:T(8,128)(2,1)} %param.19), kind=kOutput, calls=%fused_computation.18 | convolution fusion | flops 86188032 | bytes 1880256 | tf_op jit(solution)/shard_map/dot_general | solution.py:73
  11.5 7.6 %all-to-all-start = ((bf16[16,48,1152]{2,1,0:T(8,128)(2,1)}), bf16[16,48,1152]{2,1,0:T(8,128)(2,1)}, u32[]{:S(2)}, u32[]{:S(2)}) async-start(bf16[16,48,1152]{2,1,0:T(8,128)(2,1)} %bitcast.91), calls=%async_computation | async-start | bytes 3538944 | tf_op jit(solution)/shard_map/all_to_all | solution.py:74
  20.9 3.9 %fusion.113 = (bf16[1,2048,384]{2,1,0:T(8,128)(2,1)}, bf16[1,2048,384]{2,1,0:T(8,128)(2,1)}) fusion(bf16[2,2048,384]{2,1,0:T(8,128)(2,1)} %param.25), kind=kLoop, calls=%fused_computation.173 | loop fusion | bytes 6291456 | tf_op jit(solution)/shard_map/slice | solution.py:103
  24.8 2.7 %copy.124 = bf16[1,2048,384]{1,2,0:T(8,128)(2,1)} copy(bf16[1,2048,384]{2,1,0:T(8,128)(2,1)} %get-tuple-element.8) | data formatting | bytes 3145728 | tf_op jit(solution)/shard_map/slice | solution.py:103
  27.4 4.0 %fusion.114 = (bf16[1,2048,384]{2,1,0:T(8,128)(2,1)}, bf16[1,2048,384]{2,1,0:T(8,128)(2,1)}) fusion(bf16[2,2048,384]{2,1,0:T(8,128)(2,1)} %param.26), kind=kLoop, calls=%fused_computation.174 | loop fusion | bytes 6291456 | tf_op jit(solution)/shard_map/slice | solution.py:119
  31.4 2.6 %copy.128 = bf16[1,2048,384]{1,2,0:T(8,128)(2,1)} copy(bf16[1,2048,384]{2,1,0:T(8,128)(2,1)} %get-tuple-element.10) | data formatting | bytes 3145728 | tf_op jit(solution)/shard_map/slice | solution.py:119
  34.0 2.6 %copy.131 = bf16[1,2048,384]{1,2,0:T(8,128)(2,1)} copy(bf16[1,2048,384]{2,1,0:T(8,128)(2,1)} %get-tuple-element.7) | data formatting | bytes 3145728 | tf_op jit(solution)/shard_map/slice | solution.py:103
  36.6 2.7 %copy.135 = bf16[1,2048,384]{1,2,0:T(8,128)(2,1)} copy(bf16[1,2048,384]{2,1,0:T(8,128)(2,1)} %get-tuple-element.9) | data formatting | bytes 3145728 | tf_op jit(solution)/shard_map/slice | solution.py:119
  41.6 1.7 copy.138
  45.9 2.7 %fusion.12 = pred[256,2304]{0,1:T(8,128)(4,1)} fusion(s32[2304]{0:T(1024)S(1)} %iota_add_fusion, pred[2304]{0:T(1024)(128)(4,1)S(1)} %get-tuple-element.23, pred[2304]{0:T(1024)(128)(4,1)S(1)} %get-tuple-element.24), kind=kLoop, calls=%fused_computation.22 | loop fusion | flops 1179648 | bytes 603648 | tf_op jit(solution)/shard_map/jit(_where)/select_n | solution.py:138
  48.6 2.0 convolution_convert_fusion.2
  54.2 1.8 convolution_multiply_fusion.1
  57.8 2.3 fusion.28
  61.0 1.8 convolution_multiply_fusion
  64.6 2.3 fusion.29
  67.1 1.2 convolution_convert_fusion.3
  68.4 6.7 %all-to-all-start.1 = ((bf16[16,48,384]{2,1,0:T(8,128)(2,1)}), bf16[16,48,384]{2,1,0:T(8,128)(2,1)}, u32[]{:S(2)}, u32[]{:S(2)}) async-start(bf16[16,48,384]{2,1,0:T(8,128)(2,1)} %bitcast.99), calls=%async_computation.1 | async-start | bytes 1179648 | tf_op jit(solution)/shard_map/all_to_all | solution.py:130
  75.3 5.0 %fusion.117 = f32[4,256]{1,0:T(4,128)S(1)} fusion(pred[256,2304]{0,1:T(8,128)(4,1)} %fusion.12, bf16[256,4,96]{0,2,1:T(8,128)(2,1)} %bitcast.106, bf16[256,4,96]{0,2,1:T(8,128)(2,1)S(1)} %bitcast.104, bf16[2048,4,96]{0,2,1:T(8,128)(2,1)} %bitcast.93), kind=kOutput, calls=%fused_computation.177 | convolution fusion | flops 465963264 | bytes 2560000 | tf_op jit(solution)/shard_map/sub | solution.py:22
  80.2 7.7 %fusion.23 = bf16[4,96,256]{2,1,0:T(8,128)(2,1)} fusion(f32[4,256]{1,0:T(4,128)S(1)} %fusion.117, bf16[256,4,96]{0,2,1:T(8,128)(2,1)} %bitcast.108, bf16[2048,4,96]{0,2,1:T(8,128)(2,1)} %bitcast.97, pred[256,2304]{0,1:T(8,128)(4,1)} %fusion.12, bf16[256,4,96]{0,2,1:T(8,128)(2,1)} %bitcast.107, bf16[256,4,96]{0,2,1:T(8,128)(2,1)S(1)} %bitcast.105, ...), kind=kOutput, calls=%fused_computation.41 | convolution fusion | flops 924945664 | bytes 4526080 | tf_op jit(solution)/shard_map/hqk,khd->qhd/dot_general | solution.py:153
  87.9 1.4 convolution_convert_fusion.5
  89.4 3.1 %fusion.50 = f32[304,3072]{1,0:T(8,128)S(1)} fusion(bf16[384,3072]{1,0:T(8,128)(2,1)} %param.31, bf16[256,384]{0,1:T(8,128)(2,1)} %bitcast.109, bf16[48,384]{0,1:T(8,128)(2,1)S(1)} %copy.142), kind=kOutput, calls=%fused_computation.71 | convolution fusion | flops 717692928 | bytes 6328320 | tf_op jit(solution)/shard_map/dot_general | solution.py:158
  92.6 1.5 convert_element_type.142
  94.4 66.4 %all-reduce.3.cloned.1.call-done = bf16[304,3072]{1,0:T(8,128)(2,1)} async-done(((bf16[304,3072]{1,0:T(8,128)(2,1)}), bf16[304,3072]{1,0:T(8,128)(2,1)}) %all-reduce.3.cloned.1.call-update) | async-done | bytes 1867792 | tf_op jit(solution)/shard_map/psum | solution.py:165
  160.8 2.1 multiply_reduce_fusion
  163.0 3.9 %fusion.46 = f32[304,512]{1,0:T(8,128)} fusion(bf16[3072,512]{1,0:T(8,128)(2,1)} %param.33, f32[3072]{0:T(1024)S(1)} %copy-done.17, f32[304]{0:T(512)S(1)} %add_rsqrt_fusion, bf16[304,3072]{1,0:T(8,128)(2,1)S(1)} %copy-done.1), kind=kOutput, calls=%fused_computation.63 | convolution fusion | flops 960036864 | bytes 5649600 | tf_op jit(solution)/shard_map/dot_general | solution.py:170
  166.9 6.1 %convolution_convert_fusion = bf16[304,3072]{1,0:T(8,128)(2,1)} fusion(bf16[512,3072]{1,0:T(8,128)(2,1)S(1)} %copy-done, bf16[3072,512]{1,0:T(8,128)(2,1)} %param.34, f32[304,512]{1,0:T(8,128)} %fusion.46, f32[3072]{0:T(1024)S(1)} %copy-done.17, f32[304]{0:T(512)S(1)} %add_rsqrt_fusion, bf16[304,3072]{1,0:T(8,128)(2,1)} %all-reduce.3.cloned.1.call-done), kind=kOutput, calls=%fused_computation.13 | convolution fusion | flops 1918205952 | bytes 10663104 | tf_op jit(solution)/shard_map/dot_general | solution.py:173
  173.0 4.1 %copy.149 = bf16[304,3072]{0,1:T(8,128)(2,1)} copy(bf16[304,3072]{1,0:T(8,128)(2,1)} %convolution_convert_fusion) | data formatting | bytes 3735552
  179.0 3.8 %convert_element_type.143 = f32[304,3072]{1,0:T(8,128)} convert(bf16[304,3072]{1,0:T(8,128)(2,1)} %all-reduce.3.cloned.1.call-done) | non-fusion elementwise | flops 933888 | bytes 5603328 | tf_op jit(solution)/shard_map/convert_element_type | solution.py:167
  182.8 27.3 %reduce-scatter.4.cloned.1.call-done = bf16[384,304]{1,0:T(8,128)(2,1)} async-done(((bf16[3072,304]{1,0:T(8,128)(2,1)}), bf16[384,304]{1,0:T(8,128)(2,1)}) %reduce-scatter.4.cloned.1.call-update) | async-done | bytes 233488
  211.3 1.5 convolution_convert_fusion.4
  212.8 15.3 %all_to_all.52 = bf16[16,40,384]{2,1,0:T(8,128)(2,1)S(1)} all-to-all(bf16[16,40,384]{2,1,0:T(8,128)(2,1)S(1)} %bitcast.100), channel_id=1, replica_groups=mesh['req'=16,'head'=8] {'req'}, dimensions={0} | all-to-all | bytes 983040 | tf_op jit(solution)/shard_map/all_to_all | solution.py:190
  228.0 17.3 %all_to_all.53 = bf16[8,80,384]{2,1,0:T(8,128)(2,1)S(1)} all-to-all(bf16[8,80,384]{2,1,0:T(8,128)(2,1)S(1)} %bitcast.101), channel_id=1, replica_groups=mesh['req'=16,'head'=8] {'head'}, dimensions={0} | all-to-all | bytes 983040 | tf_op jit(solution)/shard_map/all_to_all | solution.py:191
  (108 shorter events, 21.0 us)
Async XLA Ops:
  6.5 160.3 %copy-start = (bf16[512,3072]{1,0:T(8,128)(2,1)S(1)}, bf16[512,3072]{1,0:T(8,128)(2,1)}, u32[]{:S(2)}) copy-start(bf16[512,3072]{1,0:T(8,128)(2,1)} %param.35) | copy-start | bytes 9437188
  8.9 2.6 %copy-start.8 = (s32[48]{0:T(128)}, s32[48]{0:T(128)S(1)}, u32[]{:S(2)}) copy-start(s32[48]{0:T(128)S(1)} %dynamic-slice_add_fusion) | copy-start | bytes 580
  11.5 37.1 %all-to-all-start = ((bf16[16,48,1152]{2,1,0:T(8,128)(2,1)}), bf16[16,48,1152]{2,1,0:T(8,128)(2,1)}, u32[]{:S(2)}, u32[]{:S(2)}) async-start(bf16[16,48,1152]{2,1,0:T(8,128)(2,1)} %bitcast.91), calls=%async_computation | async-start | bytes 3538944 | tf_op jit(solution)/shard_map/all_to_all | solution.py:74
  20.8 27.8 %copy-start.12 = (s32[96]{0:T(128)}, s32[96]{0:T(128)S(1)}, u32[]{:S(2)}) copy-start(s32[96]{0:T(128)S(1)} %eq.158) | copy-start | bytes 1156
  20.9 27.7 %copy-start.14 = (pred[96]{0:T(512)(128)(4,1)}, pred[96]{0:T(512)(128)(4,1)S(1)}, u32[]{:S(2)}) copy-start(pred[96]{0:T(512)(128)(4,1)S(1)} %and.43) | copy-start | bytes 292
  36.6 3.4 %copy-start.5 = (bf16[256,384]{1,0:T(8,128)(2,1)S(1)}, bf16[256,384]{1,0:T(8,128)(2,1)}, u32[]{:S(2)}) copy-start(bf16[256,384]{1,0:T(8,128)(2,1)} %param.23) | copy-start | bytes 589828
  36.6 4.2 %copy-start.6 = (bf16[256,384]{1,0:T(8,128)(2,1)S(1)}, bf16[256,384]{1,0:T(8,128)(2,1)}, u32[]{:S(2)}) copy-start(bf16[256,384]{1,0:T(8,128)(2,1)} %param.22) | copy-start | bytes 589828
  36.6 6.8 %copy-start.11 = (s32[2]{0:T(128)S(1)}, s32[2]{0:T(128)}, u32[]{:S(2)}) copy-start(s32[2]{0:T(128)} %param.28) | copy-start | bytes 28
  56.6 0.9 copy-start.3
  60.3 2.5 copy-start.10
  63.5 0.9 copy-start.2
  64.4 2.7 %copy-start.13 = (s32[96]{0:T(128)S(1)}, s32[96]{0:T(128)}, u32[]{:S(2)}) copy-start(s32[96]{0:T(128)} %copy-done.12) | copy-start | bytes 1156
  64.4 2.7 %copy-start.15 = (pred[96]{0:T(512)(128)(4,1)S(1)}, pred[96]{0:T(512)(128)(4,1)}, u32[]{:S(2)}) copy-start(pred[96]{0:T(512)(128)(4,1)} %copy-done.14) | copy-start | bytes 292
  64.6 10.7 %copy-start.7 = (bf16[256,384]{0,1:T(8,128)(2,1)S(1)}, bf16[256,384]{0,1:T(8,128)(2,1)}, u32[]{:S(2)}) copy-start(bf16[256,384]{0,1:T(8,128)(2,1)} %copy.139) | copy-start | bytes 589828
  68.4 19.6 %all-to-all-start.1 = ((bf16[16,48,384]{2,1,0:T(8,128)(2,1)}), bf16[16,48,384]{2,1,0:T(8,128)(2,1)}, u32[]{:S(2)}, u32[]{:S(2)}) async-start(bf16[16,48,384]{2,1,0:T(8,128)(2,1)} %bitcast.99), calls=%async_computation.1 | async-start | bytes 1179648 | tf_op jit(solution)/shard_map/all_to_all | solution.py:130
  75.0 85.8 %all-reduce.3.cloned.1.call-start = ((), (), s32[]{:S(2)}) async-start(), calls=%async_computation.5 | async-start | bytes 3735552 | tf_op jit(solution)/shard_map/psum | solution.py:165
  80.2 7.7 %copy-start.9 = (s32[48]{0:T(128)S(1)}, s32[48]{0:T(128)}, u32[]{:S(2)}) copy-start(s32[48]{0:T(128)} %copy-done.8) | copy-start | bytes 580
  89.4 3.1 %copy-start.4 = (bf16[304,384]{1,0:T(8,128)(2,1)S(1)}, bf16[304,384]{1,0:T(8,128)(2,1)}, u32[]{:S(2)}) copy-start(bf16[304,384]{1,0:T(8,128)(2,1)} %param.18) | copy-start | bytes 700420
  94.1 68.8 %copy-start.17 = (f32[3072]{0:T(1024)S(1)}, f32[3072]{0:T(1024)}, u32[]{:S(2)}) copy-start(f32[3072]{0:T(1024)} %param.32) | copy-start | bytes 36868
  94.1 116.0 %reduce-scatter.4.cloned.1.call-start = ((), (), s32[]{:S(2)}) async-start(), calls=%async_computation.6 | async-start | bytes 2654208
  160.8 2.1 copy-start.1
  177.1 0.7 copy-start.16
Sparse Core Ops, SparseCore 0:
  94.3 66.5 all-reduce.2
  177.2 32.8 reduce-scatter.3
